TPU v7x, 256 devices: a whole 4x4x8 slice. The times are simulated.
256 devices in a mesh: frame: 32 (over z, x_hi, core), head: 8 (over y, x_lo).
Axes of the slice: x: 4 (x_hi: 2, x_lo: 2; x = x_hi * 2 + x_lo), y: 4, z: 8, core: 2. Of those that a mesh axis runs over, the one named last changes fastest.
Arguments:
- query_vectors: bfloat16 [12288, 3072], P('frame', 'head'), may hold values from -17 to 17
- key_vectors: bfloat16 [12288, 3072], P('frame', 'head'), may hold values from -6 to 6
- value_vectors: bfloat16 [12288, 3072], P('frame', 'head'), may hold values from -6 to 6
- tile_mask: int32 [96, 96], replicated, may hold values from 0 to 1, as said below
- out_weight: bfloat16 [3072, 3072], P('head'), may hold values from -0.109375 to 0.109375
Outputs:
- projected: bfloat16 [12288, 3072], P(('frame', 'head'))
Inputs may be any that keep to these rules, and one draw needn't show every extreme that they name: The slab holds packed clips of whole tiles. Each clip lays its tiles out in order on a grid of latent frames by tile rows by tile columns. One clip spans 72 tiles and its latent frame holds 48 tiles, in 4 or 8 columns; every other clip has 2 to 4 rows and 2 to 4 columns, by clip. tile_mask[a, b] is 1 exactly when tiles a and b lie in the same clip and their frame, row and column indices each differ by at most 1.
All inputs are finite; a program needn't handle non-finite values.
Results may differ from a plain program's by a relative error of at most 0.02.
Values may be sent and summed in bfloat16 or wider, within the bound.
No kernel may reach another device: no remote copies, remote signals or barrier semaphores. Data moves between devices by JAX's collectives and lax.ppermute only.
A program may use at most 128 MiB of HBM per device.

v0:
```python
import math

import jax
import jax.numpy as jnp
from jax import lax
from jax.sharding import PartitionSpec as P

HD = 128
TILE = 128


NEGATIVE = -1e30


def expand_mask(tile_block, row_count, col_count):
    query_tiles, key_tiles = tile_block.shape
    tile_rows = row_count // query_tiles
    expanded = jnp.broadcast_to(
        tile_block[:, None, :, None], (query_tiles, tile_rows, key_tiles, tile_rows)
    )
    return expanded.reshape(row_count, col_count) > 0


def block_scores(query_block, key_block, allowed):
    head_count = query_block.shape[1] // HD
    query_heads = query_block.reshape(query_block.shape[0], head_count, HD)
    key_heads = key_block.reshape(key_block.shape[0], head_count, HD)
    raw_scores = jnp.einsum(
        "qhd,khd->hqk", query_heads, key_heads, preferred_element_type=jnp.float32
    ) * (1.0 / math.sqrt(HD))
    return jnp.where(allowed[None], raw_scores, NEGATIVE)


def online_update(running, key_block, value_block, allowed, query_block):
    numerator, row_top, totals = running
    scores = block_scores(query_block, key_block, allowed)
    new_top = jnp.maximum(row_top, jnp.max(scores, axis=2, keepdims=True))
    weights = jnp.where(allowed[None], jnp.exp(scores - new_top), 0.0)
    factor = jnp.exp(row_top - new_top)
    totals = totals * factor + jnp.sum(weights, axis=2, keepdims=True)
    value_heads = value_block.reshape(value_block.shape[0], row_top.shape[0], HD)
    numerator = numerator * factor + jnp.einsum(
        "hqk,khd->hqd",
        weights.astype(jnp.bfloat16),
        value_heads,
        preferred_element_type=jnp.float32,
    )
    return (numerator, new_top, totals)


def shards(query_vectors, key_vectors, value_vectors, tile_mask, out_weight):
    row_count = query_vectors.shape[0]
    channels = query_vectors.shape[1]
    head_count = channels // HD
    frame_pos = lax.axis_index("frame")
    tiles_here = row_count // TILE
    query_tiles = lax.dynamic_slice_in_dim(tile_mask, frame_pos * tiles_here, tiles_here, 0)
    initial = (
        jnp.zeros((head_count, row_count, HD), jnp.float32),
        jnp.full((head_count, row_count, 1), NEGATIVE, jnp.float32),
        jnp.zeros((head_count, row_count, 1), jnp.float32),
    )
    key_piece = lax.all_gather(key_vectors, "frame", axis=0, tiled=True)
    value_piece = lax.all_gather(value_vectors, "frame", axis=0, tiled=True)
    length = key_piece.shape[0]
    block_rows = 2 * row_count
    block_span = length // block_rows
    key_tiles = query_tiles
    key_tiles = key_tiles.reshape(tiles_here, block_span, block_rows // TILE).transpose(1, 0, 2)
    key_blocks = key_piece.reshape(block_span, block_rows, channels)
    value_blocks = value_piece.reshape(block_span, block_rows, channels)

    def advance(current, element):
        key_block, value_block, tile_block = element
        allowed = expand_mask(tile_block, row_count, block_rows)
        return (online_update(current, key_block, value_block, allowed, query_vectors), None)

    result, _ = lax.scan(advance, initial, (key_blocks, value_blocks, key_tiles))
    numerator, row_top, totals = result
    attended = (
        (numerator / totals).transpose(1, 0, 2).reshape(row_count, channels).astype(jnp.bfloat16)
    )
    return lax.psum_scatter(
        jnp.dot(attended, out_weight, preferred_element_type=jnp.float32).astype(jnp.bfloat16),
        "head",
        scatter_dimension=0,
        tiled=True,
    )


def solution(mesh):
    in_specs = (P("frame", "head"), P("frame", "head"), P("frame", "head"), P(), P("head", None))
    out_specs = P(("frame", "head"), None)
    return jax.shard_map(shards, mesh=mesh, in_specs=in_specs, out_specs=out_specs, check_vma=False)
```

profile of v0, /device:TPU:1, one launch (start us, length us, event | category | flops | bytes accessed | tf_op | source)
XLA Modules:
  0.0 568.9 jit_solution(12067339337692195843)
XLA Ops:
  11.3 107.8 %all-gather.3.cloned.1.call-done = bf16[12288,384]{1,0:T(8,128)(2,1)} async-done(((bf16[384,384]{1,0:T(8,128)(2,1)}), bf16[12288,384]{1,0:T(8,128)(2,1)}) %all-gather.3.cloned.1.call-update) | async-done | bytes 9437200 | tf_op jit(solution)/shard_map/all_gather | solution.py:63
  119.1 104.5 %all-gather.5.cloned.1.call-done = bf16[12288,384]{1,0:T(8,128)(2,1)} async-done(((bf16[384,384]{1,0:T(8,128)(2,1)}), bf16[12288,384]{1,0:T(8,128)(2,1)}) %all-gather.5.cloned.1.call-update) | async-done | bytes 9437200 | tf_op jit(solution)/shard_map/all_gather | solution.py:64
  223.6 278.3 %while.15 = (s32[]{:T(128)}, f32[3,384,128]{2,1,0:T(8,128)}, f32[3,384,1]{1,0,2:T(4,128)S(1)}, f32[3,384,1]{1,0,2:T(4,128)S(1)}, s32[16,3,6]{2,0,1:T(8,128)}, /*...) while((s32[]{:T(128)}, f32[3,384,128]{2,1,0:T(8,128)}, ...), condition=%wide.region_3.4_spmd.clone, body=%wide.region_0.3_spmd.clone.sunk | while | flops 464935680 | bytes 22782352 | solution.py:78
  228.8 3.7 fusion.33
  236.6 4.3 fusion.35
  246.0 3.7 fusion.33
  253.8 4.5 fusion.35
  263.4 3.7 fusion.33
  271.2 4.5 fusion.35
  280.8 3.7 fusion.33
  288.6 4.5 fusion.35
  298.2 3.7 fusion.33
  306.0 4.5 fusion.35
  315.7 3.7 fusion.33
  323.4 4.5 fusion.35
  333.1 3.7 fusion.33
  340.8 4.5 fusion.35
  358.2 4.5 fusion.35
  367.9 3.7 fusion.33
  375.6 4.5 fusion.35
  385.3 3.7 fusion.33
  393.0 4.5 fusion.35
  410.4 4.5 fusion.35
  420.1 3.7 fusion.33
  427.8 4.5 fusion.35
  445.2 4.5 fusion.35
  454.9 3.7 fusion.33
  462.7 4.5 fusion.35
  480.1 4.5 fusion.35
  489.7 3.7 fusion.33
  497.5 4.5 fusion.35
  506.2 56.2 %reduce-scatter.2.cloned.1.call-done = bf16[48,3072]{1,0:T(8,128)(2,1)} async-done(((bf16[384,3072]{1,0:T(8,128)(2,1)}), bf16[48,3072]{1,0:T(8,128)(2,1)}) %reduce-scatter.2.cloned.1.call-update) | async-done | bytes 294928 | tf_op jit(solution)/shard_map/reduce_scatter | solution.py:83
  (245 shorter events, 171.7 us)
Async XLA Ops:
  6.5 496.8 %copy-start = (bf16[384,3072]{1,0:T(8,128)(2,1)S(1)}, bf16[384,3072]{1,0:T(8,128)(2,1)}, u32[]{:S(2)}) copy-start(bf16[384,3072]{1,0:T(8,128)(2,1)} %param.11) | copy-start | bytes 7077892
  6.5 112.6 %all-gather.3.cloned.1.call-start = ((), (), s32[]{:S(2)}) async-start(), calls=%async_computation.1 | async-start | bytes 9732096 | tf_op jit(solution)/shard_map/all_gather | solution.py:63
  7.3 216.4 %all-gather.5.cloned.1.call-start = ((), (), s32[]{:S(2)}) async-start(), calls=%async_computation.2 | async-start | bytes 9732096 | tf_op jit(solution)/shard_map/all_gather | solution.py:64
  8.0 554.4 %reduce-scatter.2.cloned.1.call-start = ((), (), s32[]{:S(2)}) async-start(), calls=%async_computation.3 | async-start | bytes 2654208 | tf_op jit(solution)/shard_map/reduce_scatter | solution.py:83
  232.5 3.0 copy-start.1
  249.7 3.0 copy-start.1
  267.1 3.0 copy-start.1
  284.5 3.0 copy-start.1
  301.9 3.0 copy-start.1
  319.3 3.0 copy-start.1
  336.7 3.0 copy-start.1
  354.1 3.0 copy-start.1
  371.5 3.0 copy-start.1
  388.9 3.0 copy-start.1
  406.3 3.0 copy-start.1
  423.7 3.0 copy-start.1
  441.1 3.0 copy-start.1
  458.6 3.0 copy-start.1
  476.0 3.0 copy-start.1
  493.4 3.0 copy-start.1
Sparse Core Ops, SparseCore 0:
  10.1 108.9 all-gather.2
  121.9 101.6 all-gather.4
  506.3 56.0 reduce-scatter.1
where the time goes:
time: 572 us; the launch traced here: 569 us
  waiting for transfers between devices  270 us (47%)
  matrix products  132 us (23%)
  local copies, waits for them, and re-layouts  105 us (18%)
  other arithmetic  47.9 us (8%)
  between operations  13.2 us (2%)
    all_gather x1, waiting for transfers between devices, shards(): key_piece = lax.all_gather(key_vectors, 'frame', axis=0, tiled=True)  108 us
    all_gather x1, waiting for transfers between devices, shards(): value_piece = lax.all_gather(value_vectors, 'frame', axis=0, tiled=True)  104 us
    dynamic_slice x64, local copies, waits for them, and re-layouts, shards(): lax.scan(advance, initial, (key_blocks, value_blocks, key_tiles))  87.7 us
    dot_general x16, matrix products, online_update(): jnp.einsum('hqk,khd->hqd', weights.astype(jnp.bfloat16), value_heads, pre...  71.2 us
    dot_general x16, matrix products, block_scores(): jnp.einsum('qhd,khd->hqk', query_heads, key_heads, preferred_element_type...  58.4 us
    reduce_scatter x1, waiting for transfers between devices, shards(): lax.psum_scatter(jnp.dot(attended, out_weight, preferred_element_type=jnp...  56.2 us
    reduce_sum x16, other arithmetic, online_update(): totals = totals * factor + jnp.sum(weights, axis=2, keepdims=True)  47.3 us
  transfers between devices with their start and end apart: 3, of which 3 were waited for; matrix products, arithmetic and copies ran while one was open for 1% of the time, Pallas kernels for 0%

commit v1 on v0

v1 whole, which is shorter than its diff:
```python
import functools
import math

import jax
import jax.numpy as jnp
from jax import lax
from jax.experimental import pallas as pl
from jax.experimental.pallas import tpu as pltpu
from jax.sharding import PartitionSpec as P

HD = 128
TILE = 128
MAX_KEYS = 27
KEYS_PER_STEP = 3


def key_lists(tile_rows):
    row_tiles = tile_rows.shape[1]
    allowed = tile_rows > 0
    position = jnp.cumsum(allowed.astype(jnp.int32), axis=1) - 1
    counts = jnp.minimum(jnp.sum(allowed.astype(jnp.int32), axis=1), MAX_KEYS)
    slot = jnp.where(allowed & (position < MAX_KEYS), position, MAX_KEYS)
    tiles = jnp.broadcast_to(jnp.arange(row_tiles, dtype=jnp.int32), tile_rows.shape)
    lists = jnp.zeros((tile_rows.shape[0], MAX_KEYS + 1), jnp.int32)
    lists = jax.vmap(lambda l, s, t: l.at[s].set(t))(lists, slot, tiles)[:, :MAX_KEYS]
    last = jnp.take_along_axis(lists, jnp.maximum(counts - 1, 0)[:, None], axis=1)
    lists = jnp.where(jnp.arange(MAX_KEYS)[None, :] < counts[:, None], lists, last)
    return lists.reshape(-1), counts


def attention_kernel(lists_ref, counts_ref, q_ref, *refs, head_count, scale):
    key_refs = refs[:KEYS_PER_STEP]
    value_refs = refs[KEYS_PER_STEP : 2 * KEYS_PER_STEP]
    o_ref = refs[2 * KEYS_PER_STEP]
    top_ref, total_ref, acc_ref = refs[2 * KEYS_PER_STEP + 1 :]
    tile = pl.program_id(0)
    step = pl.program_id(1)

    @pl.when(step == 0)
    def _():
        top_ref[...] = jnp.full(top_ref.shape, -jnp.inf, jnp.float32)
        total_ref[...] = jnp.zeros(total_ref.shape, jnp.float32)
        acc_ref[...] = jnp.zeros(acc_ref.shape, jnp.float32)

    for j in range(KEYS_PER_STEP):

        @pl.when(step * KEYS_PER_STEP + j < counts_ref[tile])
        def _():
            for h in range(head_count):
                cols = pl.ds(h * HD, HD)
                q = q_ref[:, cols]
                k = key_refs[j][:, cols]
                s = lax.dot_general(
                    q, k, (((1,), (1,)), ((), ())), preferred_element_type=jnp.float32
                ) * scale
                old_top = top_ref[h]
                new_top = jnp.maximum(old_top, jnp.max(s, axis=1, keepdims=True))
                weights = jnp.exp(s - new_top)
                factor = jnp.exp(old_top - new_top)
                total_ref[h] = total_ref[h] * factor + jnp.sum(weights, axis=1, keepdims=True)
                acc_ref[h] = acc_ref[h] * factor + jnp.dot(
                    weights.astype(jnp.bfloat16),
                    value_refs[j][:, cols],
                    preferred_element_type=jnp.float32,
                )
                top_ref[h] = new_top

    @pl.when(step == pl.num_programs(1) - 1)
    def _():
        for h in range(head_count):
            o_ref[:, pl.ds(h * HD, HD)] = (acc_ref[h] / total_ref[h]).astype(o_ref.dtype)


def sparse_attention(query_vectors, key_piece, value_piece, lists, counts):
    row_count, channels = query_vectors.shape
    head_count = channels // HD
    query_tiles = row_count // TILE
    steps = MAX_KEYS // KEYS_PER_STEP

    def key_spec(j):
        return pl.BlockSpec(
            (TILE, channels),
            lambda i, s, lists_ref, counts_ref: (lists_ref[i * MAX_KEYS + s * KEYS_PER_STEP + j], 0),
        )

    row_spec = pl.BlockSpec((TILE, channels), lambda i, s, lists_ref, counts_ref: (i, 0))
    kernel = functools.partial(
        attention_kernel, head_count=head_count, scale=1.0 / math.sqrt(HD)
    )
    return pl.pallas_call(
        kernel,
        grid_spec=pltpu.PrefetchScalarGridSpec(
            num_scalar_prefetch=2,
            grid=(query_tiles, steps),
            in_specs=[row_spec]
            + [key_spec(j) for j in range(KEYS_PER_STEP)]
            + [key_spec(j) for j in range(KEYS_PER_STEP)],
            out_specs=row_spec,
            scratch_shapes=[
                pltpu.VMEM((head_count, TILE, 1), jnp.float32),
                pltpu.VMEM((head_count, TILE, 1), jnp.float32),
                pltpu.VMEM((head_count, TILE, HD), jnp.float32),
            ],
        ),
        out_shape=jax.ShapeDtypeStruct((row_count, channels), jnp.bfloat16),
        compiler_params=pltpu.CompilerParams(dimension_semantics=("arbitrary", "arbitrary")),
    )(lists, counts, query_vectors, *([key_piece] * KEYS_PER_STEP), *([value_piece] * KEYS_PER_STEP))


def shards(query_vectors, key_vectors, value_vectors, tile_mask, out_weight):
    row_count = query_vectors.shape[0]
    frame_pos = lax.axis_index("frame")
    tiles_here = row_count // TILE
    query_tiles = lax.dynamic_slice_in_dim(tile_mask, frame_pos * tiles_here, tiles_here, 0)
    lists, counts = key_lists(query_tiles)
    key_piece = lax.all_gather(key_vectors, "frame", axis=0, tiled=True)
    value_piece = lax.all_gather(value_vectors, "frame", axis=0, tiled=True)
    attended = sparse_attention(query_vectors, key_piece, value_piece, lists, counts)
    return lax.psum_scatter(
        jnp.dot(attended, out_weight, preferred_element_type=jnp.float32).astype(jnp.bfloat16),
        "head",
        scatter_dimension=0,
        tiled=True,
    )


def solution(mesh):
    in_specs = (P("frame", "head"), P("frame", "head"), P("frame", "head"), P(), P("head", None))
    out_specs = P(("frame", "head"), None)
    return jax.shard_map(shards, mesh=mesh, in_specs=in_specs, out_specs=out_specs, check_vma=False)
```

time: 572 us -> 352 us (0.62)
  matrix products: 132 us -> 3.76 us
  local copies, waits for them, and re-layouts: 105 us -> 15.2 us
  other arithmetic: 47.9 us -> 1.22 us
  waiting for transfers between devices: 270 us -> 298 us
  Pallas kernels: 0 us -> 17.7 us
    dot_general x32 -> x0, matrix products: 130 us -> none  [the longest x16 71.2 us: online_update(): jnp.einsum('hqk,khd->hqd', weights.astype(jnp.bfloat16), value_heads, pre...]
    dynamic_slice x65 -> x0, local copies, waits for them, and re-layouts: 88.4 us -> none  [the longest x64 87.7 us: shards(): lax.scan(advance, initial, (key_blocks, value_blocks, key_tiles))]
    reduce_sum x16 -> x1, other arithmetic: 47.3 us -> 0.82 us  [key_lists(): counts = jnp.minimum(jnp.sum(allowed.astype(jnp.int32), axis=1), MAX_KEYS)]
    reduce_scatter x1, waiting for transfers between devices: 56.2 us -> 97.3 us  [shards(): lax.psum_scatter(jnp.dot(attended, out_weight, preferred_element_type=jnp...]
    pallas_call x0 -> x1, Pallas kernels: none -> 17.7 us  [sparse_attention(): pl.pallas_call(kernel, grid_spec=pltpu.PrefetchScalarGridSpec(num_scalar_...]
    scatter x0 -> x2, local copies, waits for them, and re-layouts: none -> 13.8 us  [key_lists(): l.at[s].set(t)]
    all_gather x1, waiting for transfers between devices: 108 us -> 94.6 us  [shards(): key_piece = lax.all_gather(key_vectors, 'frame', axis=0, tiled=True)]
    gt x16 -> x0, local copies, waits for them, and re-layouts: 7.33 us -> none  [expand_mask(): return expanded.reshape(row_count, col_count) > 0]
  transfers between devices with their start and end apart: 3 -> 3, of which waited for: 3 -> 3; matrix products, arithmetic and copies ran while one was open for 1% -> 5% of each run, Pallas kernels for 0% -> 0%
where the time goes in v1:
time: 352 us; the launch traced here: 349 us
  waiting for transfers between devices  298 us (85%)
  Pallas kernels  17.7 us (5%)
  local copies, waits for them, and re-layouts  15.2 us (4%)
  between operations  13.2 us (4%)
  matrix products  3.76 us (1%)
    all_gather x1, waiting for transfers between devices, shards(): value_piece = lax.all_gather(value_vectors, 'frame', axis=0, tiled=True)  104 us
    reduce_scatter x1, waiting for transfers between devices, shards(): lax.psum_scatter(jnp.dot(attended, out_weight, preferred_element_type=jnp...  97.3 us
    all_gather x1, waiting for transfers between devices, shards(): key_piece = lax.all_gather(key_vectors, 'frame', axis=0, tiled=True)  94.6 us
    pallas_call x1, Pallas kernels, sparse_attention(): pl.pallas_call(kernel, grid_spec=pltpu.PrefetchScalarGridSpec(num_scalar_...  17.7 us
    scatter x2, local copies, waits for them, and re-layouts, key_lists(): l.at[s].set(t)  13.8 us
  transfers between devices with their start and end apart: 3, of which 3 were waited for; matrix products, arithmetic and copies ran while one was open for 5% of the time, Pallas kernels for 0%

profile of v1, /device:TPU:1, one launch (start us, length us, event | category | flops | bytes accessed | tf_op | source)
XLA Modules:
  0.0 349.0 jit_solution(9841049666005255944)
XLA Ops:
  6.5 0.0 copy-start
  6.5 0.0 all-gather.3.cloned.1.call-start
  6.5 0.7 all-gather.3.cloned.1.call-update
  7.3 0.0 all-gather.5.cloned.1.call-start
  7.3 0.7 all-gather.5.cloned.1.call-update
  8.0 0.0 reduce-scatter.2.cloned.1.call-start
  8.1 0.8 convert_reduce_fusion
  8.9 0.3 reduce_window_sum.11
  9.2 0.1 reshape.58
  9.3 0.1 reshape.60
  9.4 13.8 %scatter_fusion = s32[3,28]{1,0:T(4,128)S(1)} fusion(s32[3,28]{1,0:T(4,128)S(1)} %broadcast_in_dim.22, s32[288]{0:T(512)S(1)} %reshape.58, s32[288]{0:T(512)S(1)} %reshape.60), kind=kCustom, calls=%fused_computation.1 | custom fusion | bytes 5760 | tf_op jit(solution)/shard_map/vmap()/scatter | solution.py:25
  23.2 0.7 gather_fusion
  23.8 0.0 copy-start.1
  23.8 0.1 fusion.5
  23.9 0.6 reshape.49.lists_ref
  24.5 94.6 %all-gather.3.cloned.1.call-done.refs_0_.refs_1_.refs_2_ = bf16[12288,384]{1,0:T(8,128)(2,1)} async-done(((bf16[384,384]{1,0:T(8,128)(2,1)}), bf16[12288,384]{1,0:T(8,128)(2,1)}) %all-gather.3.cloned.1.call-update) | async-done | bytes 9437200 | tf_op jit(solution)/shard_map/all_gather | solution.py:116
  119.1 104.5 %all-gather.5.cloned.1.call-done.refs_3_.refs_4_.refs_5_ = bf16[12288,384]{1,0:T(8,128)(2,1)} async-done(((bf16[384,384]{1,0:T(8,128)(2,1)}), bf16[12288,384]{1,0:T(8,128)(2,1)}) %all-gather.5.cloned.1.call-update) | async-done | bytes 9437200 | tf_op jit(solution)/shard_map/all_gather | solution.py:117
  223.6 0.0 copy-done.1
  223.6 17.7 %shard_map.55 = bf16[384,384]{1,0:T(8,128)(2,1)} custom-call(s32[81]{0:T(128)} %reshape.49.lists_ref, s32[3]{0:T(128)} %copy-done.1, bf16[384,384]{1,0:T(8,128)(2,1)} %q_ref.1, bf16[12288,384]{1,0:T(8,128)(2,1)} %all-gather.3.cloned.1.call-done.refs_0_.refs_1_.refs_2_, bf16[12288,384]{1,0:T(8,128)(2,1)} %all-gather.3.cloned.1.call-done.refs_0_.refs_1_.refs_2_, ...), custom_call_target="tpu_custom_call" | custom-call | tf_op jit(solution)/shard_map/pallas_call | solution.py:90
  241.3 0.0 copy-done
  241.3 3.8 %convolution_convert_fusion = bf16[384,3072]{1,0:T(8,128)(2,1)} fusion(bf16[384,384]{1,0:T(8,128)(2,1)} %shard_map.55, bf16[384,3072]{1,0:T(8,128)(2,1)S(1)} %copy-done), kind=kOutput, calls=%fused_computation.2 | convolution fusion | flops 907149312 | bytes 5013504 | tf_op jit(solution)/shard_map/dot_general | solution.py:120
  245.1 0.0 reduce-scatter.2.cloned.1.call-update
  245.1 97.3 %reduce-scatter.2.cloned.1.call-done = bf16[48,3072]{1,0:T(8,128)(2,1)} async-done(((bf16[384,3072]{1,0:T(8,128)(2,1)}), bf16[48,3072]{1,0:T(8,128)(2,1)}) %reduce-scatter.2.cloned.1.call-update) | async-done | bytes 294928 | tf_op jit(solution)/shard_map/reduce_scatter | solution.py:119
  (9 shorter events, 0.1 us)
Async XLA Ops:
  6.5 234.8 %copy-start = (bf16[384,3072]{1,0:T(8,128)(2,1)S(1)}, bf16[384,3072]{1,0:T(8,128)(2,1)}, u32[]{:S(2)}) copy-start(bf16[384,3072]{1,0:T(8,128)(2,1)} %param.9) | copy-start | bytes 7077892
  6.5 112.6 %all-gather.3.cloned.1.call-start = ((), (), s32[]{:S(2)}) async-start(), calls=%async_computation.1 | async-start | bytes 9732096 | tf_op jit(solution)/shard_map/all_gather | solution.py:116
  7.3 216.4 %all-gather.5.cloned.1.call-start = ((), (), s32[]{:S(2)}) async-start(), calls=%async_computation.2 | async-start | bytes 9732096 | tf_op jit(solution)/shard_map/all_gather | solution.py:117
  8.0 334.4 %reduce-scatter.2.cloned.1.call-start = ((), (), s32[]{:S(2)}) async-start(), calls=%async_computation.3 | async-start | bytes 2654208 | tf_op jit(solution)/shard_map/reduce_scatter | solution.py:119
  23.8 199.8 %copy-start.1 = (s32[3]{0:T(128)}, s32[3]{0:T(128)S(1)}, u32[]{:S(2)}) copy-start(s32[3]{0:T(128)S(1)} %get-tuple-element.7.counts_ref) | copy-start | bytes 40
Sparse Core Ops, SparseCore 0:
  10.1 108.9 all-gather.2
  121.9 101.6 all-gather.4
  245.2 97.1 reduce-scatter.1
